TPU v7x, 32 devices: a whole 2x2x4 slice. The times are simulated.
32 devices in a mesh: ctx: 4 (over y, core), ep: 8 (over z, x).
Axes of the slice: x: 2, y: 2, z: 4, core: 2. Of those that a mesh axis runs over, the one named last changes fastest.
Arguments:
- hidden_state: bfloat16 [512, 2048], P(('ctx', 'ep')), may hold values from -200 to 200
- upstream_grad: bfloat16 [512, 2048], P(('ctx', 'ep')), may hold values from -6 to 6
- route_ids: int32 [512, 6], P(('ctx', 'ep')), may hold values from 0 to 31, all different within a row; in each aligned block of 16 rows (0 to 15, 16 to 31, ...) at most 6 rows name the same one
- route_gates: float32 [512, 6], P(('ctx', 'ep')), may hold values from 0.05 to 0.5
- norm_gain: float32 [2048], replicated, may hold values from 0.25 to 1.75
- w_gate: bfloat16 [8, 4, 1408, 2048], P('ep', 'ctx'), may hold values from -0.125 to 0.125
- w_up: bfloat16 [8, 4, 1408, 2048], P('ep', 'ctx'), may hold values from -0.125 to 0.125
- w_down: bfloat16 [8, 4, 1408, 2048], P('ep', 'ctx'), may hold values from -0.15625 to 0.15625
- out_proj: bfloat16 [2048, 2048], P('ep'), may hold values from -0.125 to 0.125
- queries: bfloat16 [512, 2048], P('ctx', 'ep'), may hold values from -12 to 12
- key_rows: bfloat16 [512, 2048], P('ctx', 'ep'), may hold values from -12 to 12
- value_rows: bfloat16 [512, 2048], P('ctx', 'ep'), may hold values from -6 to 6
Outputs:
- grad_state: bfloat16 [512, 2048], P(('ctx', 'ep'))
- grad_queries: bfloat16 [512, 2048], P('ctx', 'ep')
- grad_keys: bfloat16 [512, 2048], P('ctx', 'ep')
- grad_values: bfloat16 [512, 2048], P('ctx', 'ep')
- grad_gate: bfloat16 [8, 4, 1408, 2048], P('ep', 'ctx')
- grad_up: bfloat16 [8, 4, 1408, 2048], P('ep', 'ctx')
- grad_down: bfloat16 [8, 4, 1408, 2048], P('ep', 'ctx')
Inputs may be any that keep to these rules, and one draw needn't show every extreme that they name: `route_ids`: within the 16 tokens of one routing block no expert is named by more than 6 routes, a bound that some block reaches.
All inputs are finite; a program needn't handle non-finite values.
Results may differ from a plain program's by a relative error of at most 0.015.
Values may be sent and summed in bfloat16 or wider, within the bound.
No kernel may reach another device: no remote copies, remote signals or barrier semaphores. Data moves between devices by JAX's collectives and lax.ppermute only.
A program may use at most 128 MiB of HBM per device.

v0:
```python
import math
import jax
import jax.numpy as jnp
from jax import lax
from jax.sharding import PartitionSpec as P

HD = 128
EXP_DEV = 4
EPSILON = 1e-06
FLOOR_SCORE = -1e30
PRECISE = lax.Precision.HIGHEST


def shifted(block, axis, distance):
    devices = range(lax.axis_size(axis))
    route = [((i - distance) % len(devices), i) for i in devices]
    return lax.ppermute(block, axis, route)


def expert_pass(token_rows, grad_rows, gate_rows, up_rows, down_rows):
    contract = (((1,), (1,)), ((), ()))
    over_rows = (((0,), (0,)), ((), ()))
    pre_gate = lax.dot_general(token_rows, gate_rows, contract, preferred_element_type=jnp.float32)
    up_value = lax.dot_general(token_rows, up_rows, contract, preferred_element_type=jnp.float32)
    sigmoid = jax.nn.sigmoid(pre_gate)
    activation = (pre_gate * sigmoid * up_value).astype(jnp.bfloat16)
    act_grad = lax.dot_general(grad_rows, down_rows, contract, preferred_element_type=jnp.float32)
    up_grad = (act_grad * pre_gate * sigmoid).astype(jnp.bfloat16)
    gate_grad = (act_grad * up_value * sigmoid * (1.0 + pre_gate * (1.0 - sigmoid))).astype(
        jnp.bfloat16
    )
    partial_value = (
        jnp.dot(gate_grad, gate_rows, preferred_element_type=jnp.float32)
        + jnp.dot(up_grad, up_rows, preferred_element_type=jnp.float32)
    ).astype(jnp.bfloat16)
    gate_total = lax.dot_general(
        gate_grad, token_rows, over_rows, preferred_element_type=jnp.float32
    )
    up_total = lax.dot_general(up_grad, token_rows, over_rows, preferred_element_type=jnp.float32)
    down_total = lax.dot_general(
        activation, grad_rows, over_rows, preferred_element_type=jnp.float32
    )
    return (partial_value, gate_total, up_total, down_total)


def score_tile(query_heads, key_heads, query_first, key_first):
    scale = 1.0 / math.sqrt(query_heads.shape[2])
    raw_scores = (
        jnp.einsum("qhd,khd->hqk", query_heads, key_heads, preferred_element_type=jnp.float32)
        * scale
    )
    query_pos = query_first + jnp.arange(query_heads.shape[0], dtype=jnp.int32)
    key_pos = key_first + jnp.arange(key_heads.shape[0], dtype=jnp.int32)
    return (raw_scores, (query_pos[:, None] >= key_pos[None, :])[None, :, :])


def stats_update(state_carry, key_part, value_part, key_first, query_heads, query_first):
    row_top, row_total, weighted = state_carry
    head_count, head_size = (query_heads.shape[1], query_heads.shape[2])
    key_heads = key_part.reshape(-1, head_count, head_size)
    value_heads = value_part.reshape(-1, head_count, head_size)
    raw_scores, allowed = score_tile(query_heads, key_heads, query_first, key_first)
    new_top = jnp.maximum(row_top, jnp.max(jnp.where(allowed, raw_scores, FLOOR_SCORE), axis=2))
    weights = jnp.where(allowed, jnp.exp(raw_scores - new_top[:, :, None]), 0.0)
    row_total = jnp.sum(weights, axis=2)
    weighted = jnp.einsum(
        "hqk,khd->hqd", weights, value_heads.astype(jnp.float32), precision=PRECISE
    )
    return (new_top, row_total, weighted)


def tile_grads(
    key_part, value_part, key_first, query_heads, dout_heads, log_total, row_delta, query_first
):
    head_count, head_size = (query_heads.shape[1], query_heads.shape[2])
    scale = 1.0 / math.sqrt(head_size)
    key_heads = key_part.reshape(-1, head_count, head_size)
    value_heads = value_part.reshape(-1, head_count, head_size)
    raw_scores, allowed = score_tile(query_heads, key_heads, query_first, key_first)
    probs = jnp.where(allowed, jnp.exp(raw_scores - log_total[:, :, None]), 0.0)
    value_grad = jnp.einsum(
        "hqk,qhd->khd", probs.astype(jnp.bfloat16), dout_heads, preferred_element_type=jnp.float32
    )
    prob_grad = jnp.einsum(
        "qhd,khd->hqk", dout_heads, value_heads, preferred_element_type=jnp.float32
    )
    score_grad = (probs * (prob_grad - row_delta[:, :, None])).astype(jnp.bfloat16)
    query_grad = (
        jnp.einsum("hqk,khd->qhd", score_grad, key_heads, preferred_element_type=jnp.float32)
        * scale
    )
    key_grad = (
        jnp.einsum("hqk,qhd->khd", score_grad, query_heads, preferred_element_type=jnp.float32)
        * scale
    )
    return (query_grad, key_grad, value_grad)


def local(
    hidden_state,
    upstream_grad,
    route_ids,
    route_gates,
    norm_gain,
    w_gate,
    w_up,
    w_down,
    out_proj,
    queries,
    key_rows,
    value_rows,
):
    ep_count = lax.axis_size("ep")
    ctx_count = lax.axis_size("ctx")
    tok_dev, model_width = hidden_state.shape
    topk_count = route_ids.shape[1]
    expert_count = EXP_DEV * ep_count
    copies = ctx_count // EXP_DEV
    capacity = max(2, 2 * tok_dev * topk_count // expert_count)
    route_count = tok_dev * topk_count
    tok_ctx = queries.shape[0]
    head_count = queries.shape[1] // HD
    ctx_index = lax.axis_index("ctx")
    query_first = ctx_index * tok_ctx
    query_heads = queries.reshape(tok_ctx, head_count, HD)
    stats_init = (
        jnp.full((head_count, tok_ctx), FLOOR_SCORE, jnp.float32),
        jnp.zeros((head_count, tok_ctx), jnp.float32),
        jnp.zeros((head_count, tok_ctx, HD), jnp.float32),
    )
    softmax_stats = stats_update(
        stats_init,
        lax.all_gather(key_rows, "ctx", axis=0, tiled=True),
        lax.all_gather(value_rows, "ctx", axis=0, tiled=True),
        jnp.int32(0),
        query_heads,
        query_first,
    )
    state = hidden_state.astype(jnp.float32)
    inv_rms = lax.rsqrt(jnp.mean(state * state, axis=1, keepdims=True) + EPSILON)
    normed = (state * inv_rms * norm_gain[None, :]).astype(jnp.bfloat16)
    flat_ids = route_ids.reshape(route_count)
    matches = (flat_ids[:, None] == jnp.arange(expert_count, dtype=jnp.int32)[None, :]).astype(
        jnp.int32
    )
    earlier = jnp.cumsum(matches, axis=0) - matches
    slot_index = jnp.sum(earlier * matches, axis=1)
    slot_ids = jnp.arange(capacity, dtype=jnp.int32)
    dispatch = (
        matches.T[:, None, :] * (slot_index[None, None, :] == slot_ids[None, :, None])
    ).astype(jnp.bfloat16)
    dispatch = dispatch.reshape(ep_count, EXP_DEV, capacity, route_count)
    normed_rep = jnp.repeat(normed, topk_count, axis=0)
    upstream_rep = jnp.repeat(upstream_grad, topk_count, axis=0).astype(jnp.float32)
    scaled_grads = (route_gates.reshape(route_count, 1) * upstream_rep).astype(jnp.bfloat16)
    gate_w = w_gate[0, 0]
    up_w = w_up[0, 0]
    down_w = w_down[0, 0]
    send_rows = jnp.repeat(
        jnp.einsum(
            "jecr,rd->jecd", dispatch, normed_rep, preferred_element_type=jnp.float32
        ).astype(jnp.bfloat16),
        copies,
        axis=1,
    )
    send_grads = jnp.repeat(
        jnp.einsum(
            "jecr,rd->jecd", dispatch, scaled_grads, preferred_element_type=jnp.float32
        ).astype(jnp.bfloat16),
        copies,
        axis=1,
    )
    received = (
        lax.all_to_all(send_rows, "ep", split_axis=0, concat_axis=0, tiled=True),
        lax.all_to_all(send_grads, "ep", split_axis=0, concat_axis=0, tiled=True),
    )
    received = (
        lax.all_to_all(received[0], "ctx", split_axis=1, concat_axis=1, tiled=True),
        lax.all_to_all(received[1], "ctx", split_axis=1, concat_axis=1, tiled=True),
    )
    partial_value, gate_total, up_total, down_total = expert_pass(
        received[0].reshape(-1, model_width),
        received[1].reshape(-1, model_width),
        gate_w,
        up_w,
        down_w,
    )
    returned = lax.all_to_all(
        partial_value.reshape(ep_count, ctx_count, capacity, model_width),
        "ctx",
        split_axis=1,
        concat_axis=1,
        tiled=True,
    )
    returned = lax.all_to_all(returned, "ep", split_axis=0, concat_axis=0, tiled=True)
    summed = jnp.sum(
        returned.reshape(ep_count, EXP_DEV, copies, capacity, model_width).astype(jnp.float32),
        axis=2,
    )
    d_routes = jnp.einsum("jecd,jecr->rd", summed, dispatch.astype(jnp.float32), precision=PRECISE)
    d_normed = jnp.sum(d_routes.reshape(tok_dev, topk_count, model_width), axis=1)
    scaled_norm = norm_gain[None, :] * d_normed
    projection = jnp.mean(state * scaled_norm, axis=1, keepdims=True)
    grad_state = (
        upstream_grad.astype(jnp.float32)
        + inv_rms * scaled_norm
        - state * inv_rms * inv_rms * inv_rms * projection
    ).astype(jnp.bfloat16)
    dout = lax.dot_general(
        lax.all_gather(grad_state, "ep", axis=0, tiled=True),
        out_proj,
        (((1,), (1,)), ((), ())),
        preferred_element_type=jnp.float32,
    ).astype(jnp.bfloat16)
    dout_heads = dout.reshape(tok_ctx, head_count, HD)
    row_top, row_total, weighted = softmax_stats
    log_total = row_top + jnp.log(row_total)
    attn_out = weighted / row_total[:, :, None]
    row_delta = jnp.einsum(
        "qhd,hqd->hq", dout_heads.astype(jnp.float32), attn_out, precision=PRECISE
    )
    query_zero = jnp.zeros((tok_ctx, head_count, HD), jnp.float32)

    def cycle_turn(turn_index, cycle_carry):
        query_pair, moving_grad, moving_stats, key_value_acc = cycle_carry
        source_dev = (ctx_index - turn_index) % ctx_count
        query_part, key_part, value_part = tile_grads(
            key_rows,
            value_rows,
            query_first,
            query_pair[0],
            query_pair[1],
            moving_stats[0],
            moving_stats[1],
            source_dev * tok_ctx,
        )
        key_value_acc = key_value_acc + jnp.stack([key_part, value_part])
        moving_grad = moving_grad + query_part
        query_pair = shifted(query_pair, "ctx", 1)
        moving_grad, moving_stats = shifted((moving_grad, moving_stats), "ctx", 1)
        return (query_pair, moving_grad, moving_stats, key_value_acc)

    query_pair_init = jnp.stack([query_heads, dout_heads])
    stats_pair = jnp.stack([log_total, row_delta])
    acc_init = jnp.zeros((2, tok_ctx, head_count, HD), jnp.float32)
    pair_final, query_grad, stats_final, key_value_grad = lax.fori_loop(
        0, ctx_count, cycle_turn, (query_pair_init, query_zero, stats_pair, acc_init)
    )
    flat_width = head_count * HD
    grad_queries = query_grad.reshape(tok_ctx, flat_width).astype(jnp.bfloat16)
    grad_keys = key_value_grad[0].reshape(tok_ctx, flat_width).astype(jnp.bfloat16)
    grad_values = key_value_grad[1].reshape(tok_ctx, flat_width).astype(jnp.bfloat16)
    return (
        grad_state,
        grad_queries,
        grad_keys,
        grad_values,
        gate_total.astype(jnp.bfloat16)[None, None],
        up_total.astype(jnp.bfloat16)[None, None],
        down_total.astype(jnp.bfloat16)[None, None],
    )


def solution(mesh):
    placed = (
        P(("ctx", "ep"), None),
        P(("ctx", "ep"), None),
        P(("ctx", "ep"), None),
        P(("ctx", "ep"), None),
        P(),
        P("ep", "ctx", None, None),
        P("ep", "ctx", None, None),
        P("ep", "ctx", None, None),
        P("ep", None),
        P("ctx", "ep"),
        P("ctx", "ep"),
        P("ctx", "ep"),
    )
    return jax.shard_map(
        local,
        mesh=mesh,
        in_specs=placed,
        out_specs=(
            P(("ctx", "ep"), None),
            P("ctx", "ep"),
            P("ctx", "ep"),
            P("ctx", "ep"),
            P("ep", "ctx", None, None),
            P("ep", "ctx", None, None),
            P("ep", "ctx", None, None),
        ),
        check_vma=False,
    )
```

profile of v0, /device:TPU:0, one launch (start us, length us, event | category | flops | bytes accessed | tf_op | source)
XLA Modules:
  0.0 223.2 jit_solution(10638249920993625415)
XLA Ops:
  4.6 1.5 copy.110
  6.1 7.3 %all-to-all-start.2 = ((bf16[8,4,6,2048]{3,1,2,0:T(4,128)(2,1)}), bf16[8,4,6,2048]{3,1,2,0:T(4,128)(2,1)}, u32[]{:S(2)}, u32[]{:S(2)}) async-start(bf16[8,4,6,2048]{3,1,2,0:T(4,128)(2,1)} %copy.110), calls=%async_computation.2 | async-start | bytes 1572864 | tf_op jit(solution)/shard_map/all_to_all | solution.py:174
  14.2 1.5 copy.107
  15.7 17.9 %all-to-all-done.2 = bf16[8,4,6,2048]{3,1,2,0:T(4,128)(2,1)} async-done(((bf16[8,4,6,2048]{3,1,2,0:T(4,128)(2,1)}), bf16[8,4,6,2048]{3,1,2,0:T(4,128)(2,1)}, u32[]{:S(2)}, u32[]{:S(2)}) %all-to-all-start.2) | async-done | bytes 786464 | tf_op jit(solution)/shard_map/all_to_all | solution.py:174
  33.6 3.6 %all-to-all-start = ((bf16[8,4,6,2048]{3,1,2,0:T(4,128)(2,1)}), bf16[8,4,6,2048]{3,1,2,0:T(4,128)(2,1)S(1)}, u32[]{:S(2)}, u32[]{:S(2)}) async-start(bf16[8,4,6,2048]{3,1,2,0:T(4,128)(2,1)} %copy.107), calls=%async_computation | async-start | bytes 1572864 | tf_op jit(solution)/shard_map/all_to_all | solution.py:175
  37.2 2.5 %copy.111 = bf16[8,4,6,2048]{3,0,2,1:T(8,128)(2,1)} copy(bf16[8,4,6,2048]{3,1,2,0:T(4,128)(2,1)} %all-to-all-done.2) | data formatting | bytes 1572864 | tf_op jit(solution)/shard_map/all_to_all | solution.py:174
  39.7 17.9 %all-to-all-done = bf16[8,4,6,2048]{3,1,2,0:T(4,128)(2,1)S(1)} async-done(((bf16[8,4,6,2048]{3,1,2,0:T(4,128)(2,1)}), bf16[8,4,6,2048]{3,1,2,0:T(4,128)(2,1)S(1)}, u32[]{:S(2)}, u32[]{:S(2)}) %all-to-all-start) | async-done | bytes 786464 | tf_op jit(solution)/shard_map/all_to_all | solution.py:175
  57.6 3.5 %all-to-all-start.3 = ((bf16[8,4,6,2048]{3,0,2,1:T(8,128)(2,1)}), bf16[8,4,6,2048]{3,0,2,1:T(8,128)(2,1)S(1)}, u32[]{:S(2)}, u32[]{:S(2)}) async-start(bf16[8,4,6,2048]{3,0,2,1:T(8,128)(2,1)} %copy.111), calls=%async_computation.3 | async-start | bytes 1572864 | tf_op jit(solution)/shard_map/all_to_all | solution.py:178
  61.4 13.6 %all_gather.11 = bf16[512,256]{0,1:T(8,128)(2,1)S(1)} all-gather(bf16[128,256]{0,1:T(8,128)(2,1)S(1)} %copy.121), channel_id=1, replica_groups=mesh['ctx'=4,'ep'=8] {'ctx'}, dimensions={0}, use_global_device_ids=true | all-gather | bytes 327680 | tf_op jit(solution)/shard_map/all_gather | solution.py:134
  76.3 4.2 %all-to-all-start.1 = ((bf16[8,4,6,2048]{3,0,2,1:T(8,128)(2,1)}), bf16[8,4,6,2048]{3,0,2,1:T(8,128)(2,1)}, u32[]{:S(2)}, u32[]{:S(2)}) async-start(bf16[8,4,6,2048]{3,0,2,1:T(8,128)(2,1)} %copy.108), calls=%async_computation.1 | async-start | bytes 1572864 | tf_op jit(solution)/shard_map/all_to_all | solution.py:179
  80.5 13.9 %all_gather.10 = bf16[512,256]{0,1:T(8,128)(2,1)S(1)} all-gather(bf16[128,256]{0,1:T(8,128)(2,1)S(1)} %copy.118), channel_id=1, replica_groups=mesh['ctx'=4,'ep'=8] {'ctx'}, dimensions={0}, use_global_device_ids=true | all-gather | bytes 327680 | tf_op jit(solution)/shard_map/all_gather | solution.py:133
  98.0 1.6 copy.109
  100.8 4.7 %fusion.28 = f32[192,1408]{1,0:T(8,128)S(1)} fusion(bf16[192,2048]{1,0:T(8,128)(2,1)S(1)} %copy-done.6, bf16[1,1,1408,2048]{3,2,1,0:T(8,128)(2,1)} %param.19), kind=kOutput, calls=%fused_computation.42 | convolution fusion | flops 1107296256 | bytes 7634944 | tf_op jit(solution)/shard_map/dot_general | solution.py:23
  105.5 5.1 %fusion.32 = f32[192,1408]{1,0:T(8,128)S(1)} fusion(bf16[192,2048]{1,0:T(8,128)(2,1)S(1)} %copy-done.6, bf16[1,1,1408,2048]{3,2,1,0:T(8,128)(2,1)} %param.20), kind=kOutput, calls=%fused_computation.46 | convolution fusion | flops 1107296256 | bytes 7634944 | tf_op jit(solution)/shard_map/dot_general | solution.py:24
  110.7 5.3 %multiply_convert_fusion.1 = (bf16[192,1408]{1,0:T(8,128)(2,1)S(1)}, bf16[192,1408]{1,0:T(8,128)(2,1)S(1)}) fusion(f32[192,1408]{1,0:T(8,128)S(1)} %fusion.28, f32[192,1408]{1,0:T(8,128)S(1)} %fusion.32, bf16[192,2048]{1,0:T(8,128)(2,1)S(1)} %copy-done.8, bf16[1,1,1408,2048]{3,2,1,0:T(8,128)(2,1)} %param.21), kind=kOutput, calls=%fused_computation.62 | convolution fusion | flops 1110810624 | bytes 9797632 | tf_op jit(solution)/shard_map/dot_general | solution.py:27
  117.5 2.3 %fusion.39 = bf16[192,2048]{1,0:T(8,128)(2,1)} fusion(f32[192,2048]{1,0:T(8,128)S(1)} %fusion.26, bf16[192,1408]{1,0:T(8,128)(2,1)S(1)} %get-tuple-element.317, bf16[1,1,1408,2048]{3,2,1,0:T(8,128)(2,1)S(1)} %bitcast.175), kind=kOutput, calls=%fused_computation.51 | convolution fusion | flops 1108082688 | bytes 8667136 | tf_op jit(solution)/shard_map/dot_general | solution.py:34
  122.5 3.5 %all-to-all-start.4 = ((bf16[8,4,6,2048]{3,0,2,1:T(8,128)(2,1)}), bf16[8,4,6,2048]{3,0,2,1:T(8,128)(2,1)S(1)}, u32[]{:S(2)}, u32[]{:S(2)}) async-start(bf16[8,4,6,2048]{3,0,2,1:T(8,128)(2,1)} %copy.113), calls=%async_computation.4 | async-start | bytes 1572864 | tf_op jit(solution)/shard_map/all_to_all | solution.py:188
  126.3 11.3 %all-to-all-done.4 = bf16[8,4,6,2048]{3,0,2,1:T(8,128)(2,1)S(1)} async-done(((bf16[8,4,6,2048]{3,0,2,1:T(8,128)(2,1)}), bf16[8,4,6,2048]{3,0,2,1:T(8,128)(2,1)S(1)}, u32[]{:S(2)}, u32[]{:S(2)}) %all-to-all-start.4) | async-done | bytes 786464 | tf_op jit(solution)/shard_map/all_to_all | solution.py:188
  137.6 1.5 copy.114
  139.1 3.8 %all-to-all-start.5 = ((bf16[8,4,6,2048]{3,1,2,0:T(4,128)(2,1)}), bf16[8,4,6,2048]{3,1,2,0:T(4,128)(2,1)S(1)}, u32[]{:S(2)}, u32[]{:S(2)}) async-start(bf16[8,4,6,2048]{3,1,2,0:T(4,128)(2,1)} %copy.114), calls=%async_computation.5 | async-start | bytes 1572864 | tf_op jit(solution)/shard_map/all_to_all | solution.py:195
  143.0 5.6 %fusion.24 = bf16[1,1,1408,2048]{3,2,1,0:T(8,128)(2,1)} fusion(bf16[192,1408]{1,0:T(8,128)(2,1)} %copy-done.22, bf16[192,2048]{1,0:T(8,128)(2,1)} %reshape.238), kind=kOutput, calls=%fused_computation.38 | convolution fusion | flops 1110179840 | bytes 7094272 | tf_op jit(solution)/shard_map/dot_general | solution.py:39
  148.6 4.2 %fusion.23 = bf16[1,1,1408,2048]{3,2,1,0:T(8,128)(2,1)} fusion(bf16[192,1408]{1,0:T(8,128)(2,1)S(1)} %copy-done.24, bf16[192,2048]{1,0:T(8,128)(2,1)S(1)} %copy-done.7), kind=kOutput, calls=%fused_computation.37 | convolution fusion | flops 1110179840 | bytes 7094272 | tf_op jit(solution)/shard_map/dot_general | solution.py:36
  152.9 4.3 %fusion.25 = bf16[1,1,1408,2048]{3,2,1,0:T(8,128)(2,1)} fusion(bf16[192,2048]{1,0:T(8,128)(2,1)S(1)} %copy-done.9, f32[192,1408]{1,0:T(8,128)S(1)} %copy-done.21, f32[192,1408]{1,0:T(8,128)S(1)} %copy-done.19), kind=kOutput, calls=%fused_computation.39 | convolution fusion | flops 1111801856 | bytes 8716288 | tf_op jit(solution)/shard_map/dot_general | solution.py:40
  157.2 5.5 %all-to-all-done.5 = bf16[8,4,6,2048]{3,1,2,0:T(4,128)(2,1)S(1)} async-done(((bf16[8,4,6,2048]{3,1,2,0:T(4,128)(2,1)}), bf16[8,4,6,2048]{3,1,2,0:T(4,128)(2,1)S(1)}, u32[]{:S(2)}, u32[]{:S(2)}) %all-to-all-start.5) | async-done | bytes 786464 | tf_op jit(solution)/shard_map/all_to_all | solution.py:195
  163.6 31.4 %all_gather.9 = bf16[128,2048]{1,0:T(8,128)(2,1)S(1)} all-gather(bf16[16,2048]{1,0:T(8,128)(2,1)S(1)} %fusion.63), channel_id=1, replica_groups=mesh['ctx'=4,'ep'=8] {'ep'}, dimensions={0}, use_global_device_ids=true | all-gather | bytes 589824 | tf_op jit(solution)/shard_map/all_gather | solution.py:210
  196.6 25.1 %while.22 = (s32[]{:T(128)}, bf16[2,128,2,128]{3,1,2,0:T(8,128)(2,1)S(1)}, f32[128,2,128]{2,0,1:T(8,128)S(1)}, f32[2,2,128]{2,1,0:T(2,128)S(1)}, f32[2,128,2,128...) while((s32[]{:T(128)}, ...), condition=%wide.region_8.9_spmd.clone, body=%wide.region_7.8_spmd.clone.sunk | while | flops 42483984 | bytes 3723668 | solution.py:246
  199.7 2.9 %collective-permute-done.1 = f32[128,2,128]{2,0,1:T(8,128)S(1)} collective-permute-done((f32[128,2,128]{2,0,1:T(8,128)S(1)}, f32[128,2,128]{2,0,1:T(8,128)S(1)}, u32[]{:S(2)}, u32[]{:S(2)}) %collective-permute-start.1) | collective-permute-done | bytes 131104 | tf_op jit(solution)/shard_map/while/body/eval_jaxpr/ppermute | solution.py:17
  202.6 1.5 collective-permute-start
  205.6 3.6 %collective-permute-done.1 = f32[128,2,128]{2,0,1:T(8,128)S(1)} collective-permute-done((f32[128,2,128]{2,0,1:T(8,128)S(1)}, f32[128,2,128]{2,0,1:T(8,128)S(1)}, u32[]{:S(2)}, u32[]{:S(2)}) %collective-permute-start.1) | collective-permute-done | bytes 131104 | tf_op jit(solution)/shard_map/while/body/eval_jaxpr/ppermute | solution.py:17
  212.2 2.9 %collective-permute-done.1 = f32[128,2,128]{2,0,1:T(8,128)S(1)} collective-permute-done((f32[128,2,128]{2,0,1:T(8,128)S(1)}, f32[128,2,128]{2,0,1:T(8,128)S(1)}, u32[]{:S(2)}, u32[]{:S(2)}) %collective-permute-start.1) | collective-permute-done | bytes 131104 | tf_op jit(solution)/shard_map/while/body/eval_jaxpr/ppermute | solution.py:17
  215.1 1.5 collective-permute-start
  218.1 3.6 %collective-permute-done.1 = f32[128,2,128]{2,0,1:T(8,128)S(1)} collective-permute-done((f32[128,2,128]{2,0,1:T(8,128)S(1)}, f32[128,2,128]{2,0,1:T(8,128)S(1)}, u32[]{:S(2)}, u32[]{:S(2)}) %collective-permute-start.1) | collective-permute-done | bytes 131104 | tf_op jit(solution)/shard_map/while/body/eval_jaxpr/ppermute | solution.py:17
  (188 shorter events, 28.2 us)
Async XLA Ops:
  0.6 194.4 %copy-start = (bf16[256,2048]{1,0:T(8,128)(2,1)S(1)}, bf16[256,2048]{1,0:T(8,128)(2,1)}, u32[]{:S(2)}) copy-start(bf16[256,2048]{1,0:T(8,128)(2,1)} %param.22) | copy-start | bytes 3145732
  4.6 8.8 %copy-start.17 = (f32[16,6]{0,1:T(8,128)S(1)}, f32[16,6]{0,1:T(8,128)}, u32[]{:S(2)}) copy-start(f32[16,6]{0,1:T(8,128)} %param.17) | copy-start | bytes 1156
  4.6 9.0 %copy-start.11 = (bf16[16,2048]{1,0:T(8,128)(2,1)S(1)}, bf16[16,2048]{1,0:T(8,128)(2,1)}, u32[]{:S(2)}) copy-start(bf16[16,2048]{1,0:T(8,128)(2,1)} %param.15) | copy-start | bytes 196612
  6.1 27.6 %all-to-all-start.2 = ((bf16[8,4,6,2048]{3,1,2,0:T(4,128)(2,1)}), bf16[8,4,6,2048]{3,1,2,0:T(4,128)(2,1)}, u32[]{:S(2)}, u32[]{:S(2)}) async-start(bf16[8,4,6,2048]{3,1,2,0:T(4,128)(2,1)} %copy.110), calls=%async_computation.2 | async-start | bytes 1572864 | tf_op jit(solution)/shard_map/all_to_all | solution.py:174
  33.6 23.9 %all-to-all-start = ((bf16[8,4,6,2048]{3,1,2,0:T(4,128)(2,1)}), bf16[8,4,6,2048]{3,1,2,0:T(4,128)(2,1)S(1)}, u32[]{:S(2)}, u32[]{:S(2)}) async-start(bf16[8,4,6,2048]{3,1,2,0:T(4,128)(2,1)} %copy.107), calls=%async_computation | async-start | bytes 1572864 | tf_op jit(solution)/shard_map/all_to_all | solution.py:175
  37.2 23.9 %copy-start.2 = (bf16[128,256]{1,0:T(8,128)(2,1)S(1)}, bf16[128,256]{1,0:T(8,128)(2,1)}, u32[]{:S(2)}) copy-start(bf16[128,256]{1,0:T(8,128)(2,1)} %param.24) | copy-start | bytes 196612
  37.2 24.0 %copy-start.1 = (bf16[128,256]{1,0:T(8,128)(2,1)S(1)}, bf16[128,256]{1,0:T(8,128)(2,1)}, u32[]{:S(2)}) copy-start(bf16[128,256]{1,0:T(8,128)(2,1)} %param.25) | copy-start | bytes 196612
  57.6 18.7 %all-to-all-start.3 = ((bf16[8,4,6,2048]{3,0,2,1:T(8,128)(2,1)}), bf16[8,4,6,2048]{3,0,2,1:T(8,128)(2,1)S(1)}, u32[]{:S(2)}, u32[]{:S(2)}) async-start(bf16[8,4,6,2048]{3,0,2,1:T(8,128)(2,1)} %copy.111), calls=%async_computation.3 | async-start | bytes 1572864 | tf_op jit(solution)/shard_map/all_to_all | solution.py:178
  75.0 19.5 %copy-start.10 = (bf16[128,256]{1,0:T(8,128)(2,1)S(1)}, bf16[128,256]{1,0:T(8,128)(2,1)}, u32[]{:S(2)}) copy-start(bf16[128,256]{1,0:T(8,128)(2,1)} %param.23) | copy-start | bytes 196612
  76.3 21.7 %all-to-all-start.1 = ((bf16[8,4,6,2048]{3,0,2,1:T(8,128)(2,1)}), bf16[8,4,6,2048]{3,0,2,1:T(8,128)(2,1)}, u32[]{:S(2)}, u32[]{:S(2)}) async-start(bf16[8,4,6,2048]{3,0,2,1:T(8,128)(2,1)} %copy.108), calls=%async_computation.1 | async-start | bytes 1572864 | tf_op jit(solution)/shard_map/all_to_all | solution.py:179
  105.5 10.5 %slice-start = ((s8[5767168]{0:T(1024)(128)(4,1)}), s8[4194304]{0:T(1024)(128)(4,1)S(1)}, s32[]{:S(2)}) async-start(s8[5767168]{0:T(1024)(128)(4,1)} %bitcast.172), calls=%async_computation.6 | async-start | bytes 8388608
  105.5 12.0 %slice-start.2 = ((s8[5767168]{0:T(1024)(128)(4,1)}), s8[4194304]{0:T(1024)(128)(4,1)S(1)}, s32[]{:S(2)}) async-start(s8[5767168]{0:T(1024)(128)(4,1)} %bitcast.174), calls=%async_computation.8 | async-start | bytes 8388608
  122.5 15.1 %all-to-all-start.4 = ((bf16[8,4,6,2048]{3,0,2,1:T(8,128)(2,1)}), bf16[8,4,6,2048]{3,0,2,1:T(8,128)(2,1)S(1)}, u32[]{:S(2)}, u32[]{:S(2)}) async-start(bf16[8,4,6,2048]{3,0,2,1:T(8,128)(2,1)} %copy.113), calls=%async_computation.4 | async-start | bytes 1572864 | tf_op jit(solution)/shard_map/all_to_all | solution.py:188
  126.3 16.6 %copy-start.16 = (s32[16,6]{0,1:T(8,128)S(1)}, s32[16,6]{0,1:T(8,128)}, u32[]{:S(2)}) copy-start(s32[16,6]{0,1:T(8,128)} %param.16) | copy-start | bytes 1156
  139.1 23.6 %all-to-all-start.5 = ((bf16[8,4,6,2048]{3,1,2,0:T(4,128)(2,1)}), bf16[8,4,6,2048]{3,1,2,0:T(4,128)(2,1)S(1)}, u32[]{:S(2)}, u32[]{:S(2)}) async-start(bf16[8,4,6,2048]{3,1,2,0:T(4,128)(2,1)} %copy.114), calls=%async_computation.5 | async-start | bytes 1572864 | tf_op jit(solution)/shard_map/all_to_all | solution.py:195
  152.9 10.5 %copy-start.5 = (bf16[16,2048]{1,0:T(8,128)(2,1)S(1)}, bf16[16,2048]{1,0:T(8,128)(2,1)}, u32[]{:S(2)}) copy-start(bf16[16,2048]{1,0:T(8,128)(2,1)} %param.14) | copy-start | bytes 196612
  152.9 10.5 %copy-start.15 = (f32[2048]{0:T(1024)S(1)}, f32[2048]{0:T(1024)}, u32[]{:S(2)}) copy-start(f32[2048]{0:T(1024)} %param.18) | copy-start | bytes 24580
  152.9 10.6 %copy-start.12 = (bf16[16,2048]{1,0:T(8,128)(2,1)S(1)}, bf16[16,2048]{1,0:T(8,128)(2,1)}, u32[]{:S(2)}) copy-start(bf16[16,2048]{1,0:T(8,128)(2,1)} %param.15) | copy-start | bytes 196612
  163.4 32.4 %copy-start.14 = (bf16[128,256]{0,1:T(8,128)(2,1)S(1)}, bf16[128,256]{0,1:T(8,128)(2,1)}, u32[]{:S(2)}) copy-start(bf16[128,256]{0,1:T(8,128)(2,1)} %copy.116) | copy-start | bytes 196612
  163.6 32.3 %copy-start.13 = (bf16[16,2048]{1,0:T(8,128)(2,1)}, bf16[16,2048]{1,0:T(8,128)(2,1)S(1)}, u32[]{:S(2)}) copy-start(bf16[16,2048]{1,0:T(8,128)(2,1)S(1)} %fusion.63) | copy-start | bytes 196612
  196.6 3.1 %collective-permute-start.2 = (f32[2,2,128]{2,1,0:T(2,128)S(1)}, f32[2,2,128]{2,1,0:T(2,128)S(1)}, u32[]{:S(2)}, u32[]{:S(2)}) collective-permute-start(f32[2,2,128]{2,1,0:T(2,128)S(1)} %copy.187), channel_id=1, source_target_pairs={{24,0},{0,8},{8,16},{16,24},{25,1},{1,9},{9,17},{17,25},{26,2},{2,... | collective-permute-start | bytes 6152 | tf_op jit(solution)/shard_map/while/body/eval_jaxpr/ppermute | solution.py:17
  196.7 5.9 %collective-permute-start = (bf16[2,128,2,128]{3,1,2,0:T(8,128)(2,1)S(1)}, bf16[2,128,2,128]{3,1,2,0:T(8,128)(2,1)S(1)}, u32[]{:S(2)}, u32[]{:S(2)}) collective-permute-start(bf16[2,128,2,128]{3,1,2,0:T(8,128)(2,1)S(1)} %copy.185), channel_id=1, source_target_pairs={{24,0},{0,8},{8,16},{16,24},{25,1},{1,9},{9,17},{17,25},{26,2},{2,... | collective-permute-start | bytes 393224 | tf_op jit(solution)/shard_map/while/body/eval_jaxpr/ppermute | solution.py:17
  198.1 4.5 %collective-permute-start.1 = (f32[128,2,128]{2,0,1:T(8,128)S(1)}, f32[128,2,128]{2,0,1:T(8,128)S(1)}, u32[]{:S(2)}, u32[]{:S(2)}) collective-permute-start(f32[128,2,128]{2,0,1:T(8,128)S(1)} %fusion.130), channel_id=1, source_target_pairs={{24,0},{0,8},{8,16},{16,24},{25,1},{1,9},{9,17},{17,25},{26,2},{2,... | collective-permute-start | bytes 393224 | tf_op jit(solution)/shard_map/while/body/eval_jaxpr/ppermute | solution.py:17
  202.5 3.0 %collective-permute-start.2 = (f32[2,2,128]{2,1,0:T(2,128)S(1)}, f32[2,2,128]{2,1,0:T(2,128)S(1)}, u32[]{:S(2)}, u32[]{:S(2)}) collective-permute-start(f32[2,2,128]{2,1,0:T(2,128)S(1)} %copy.187), channel_id=1, source_target_pairs={{24,0},{0,8},{8,16},{16,24},{25,1},{1,9},{9,17},{17,25},{26,2},{2,... | collective-permute-start | bytes 6152 | tf_op jit(solution)/shard_map/while/body/eval_jaxpr/ppermute | solution.py:17
  202.6 6.6 %collective-permute-start = (bf16[2,128,2,128]{3,1,2,0:T(8,128)(2,1)S(1)}, bf16[2,128,2,128]{3,1,2,0:T(8,128)(2,1)S(1)}, u32[]{:S(2)}, u32[]{:S(2)}) collective-permute-start(bf16[2,128,2,128]{3,1,2,0:T(8,128)(2,1)S(1)} %copy.185), channel_id=1, source_target_pairs={{24,0},{0,8},{8,16},{16,24},{25,1},{1,9},{9,17},{17,25},{26,2},{2,... | collective-permute-start | bytes 393224 | tf_op jit(solution)/shard_map/while/body/eval_jaxpr/ppermute | solution.py:17
  204.7 4.4 %collective-permute-start.1 = (f32[128,2,128]{2,0,1:T(8,128)S(1)}, f32[128,2,128]{2,0,1:T(8,128)S(1)}, u32[]{:S(2)}, u32[]{:S(2)}) collective-permute-start(f32[128,2,128]{2,0,1:T(8,128)S(1)} %fusion.130), channel_id=1, source_target_pairs={{24,0},{0,8},{8,16},{16,24},{25,1},{1,9},{9,17},{17,25},{26,2},{2,... | collective-permute-start | bytes 393224 | tf_op jit(solution)/shard_map/while/body/eval_jaxpr/ppermute | solution.py:17
  209.2 3.0 %collective-permute-start.2 = (f32[2,2,128]{2,1,0:T(2,128)S(1)}, f32[2,2,128]{2,1,0:T(2,128)S(1)}, u32[]{:S(2)}, u32[]{:S(2)}) collective-permute-start(f32[2,2,128]{2,1,0:T(2,128)S(1)} %copy.187), channel_id=1, source_target_pairs={{24,0},{0,8},{8,16},{16,24},{25,1},{1,9},{9,17},{17,25},{26,2},{2,... | collective-permute-start | bytes 6152 | tf_op jit(solution)/shard_map/while/body/eval_jaxpr/ppermute | solution.py:17
  209.2 5.9 %collective-permute-start = (bf16[2,128,2,128]{3,1,2,0:T(8,128)(2,1)S(1)}, bf16[2,128,2,128]{3,1,2,0:T(8,128)(2,1)S(1)}, u32[]{:S(2)}, u32[]{:S(2)}) collective-permute-start(bf16[2,128,2,128]{3,1,2,0:T(8,128)(2,1)S(1)} %copy.185), channel_id=1, source_target_pairs={{24,0},{0,8},{8,16},{16,24},{25,1},{1,9},{9,17},{17,25},{26,2},{2,... | collective-permute-start | bytes 393224 | tf_op jit(solution)/shard_map/while/body/eval_jaxpr/ppermute | solution.py:17
  210.6 4.4 %collective-permute-start.1 = (f32[128,2,128]{2,0,1:T(8,128)S(1)}, f32[128,2,128]{2,0,1:T(8,128)S(1)}, u32[]{:S(2)}, u32[]{:S(2)}) collective-permute-start(f32[128,2,128]{2,0,1:T(8,128)S(1)} %fusion.130), channel_id=1, source_target_pairs={{24,0},{0,8},{8,16},{16,24},{25,1},{1,9},{9,17},{17,25},{26,2},{2,... | collective-permute-start | bytes 393224 | tf_op jit(solution)/shard_map/while/body/eval_jaxpr/ppermute | solution.py:17
  215.1 3.0 %collective-permute-start.2 = (f32[2,2,128]{2,1,0:T(2,128)S(1)}, f32[2,2,128]{2,1,0:T(2,128)S(1)}, u32[]{:S(2)}, u32[]{:S(2)}) collective-permute-start(f32[2,2,128]{2,1,0:T(2,128)S(1)} %copy.187), channel_id=1, source_target_pairs={{24,0},{0,8},{8,16},{16,24},{25,1},{1,9},{9,17},{17,25},{26,2},{2,... | collective-permute-start | bytes 6152 | tf_op jit(solution)/shard_map/while/body/eval_jaxpr/ppermute | solution.py:17
  215.1 6.6 %collective-permute-start = (bf16[2,128,2,128]{3,1,2,0:T(8,128)(2,1)S(1)}, bf16[2,128,2,128]{3,1,2,0:T(8,128)(2,1)S(1)}, u32[]{:S(2)}, u32[]{:S(2)}) collective-permute-start(bf16[2,128,2,128]{3,1,2,0:T(8,128)(2,1)S(1)} %copy.185), channel_id=1, source_target_pairs={{24,0},{0,8},{8,16},{16,24},{25,1},{1,9},{9,17},{17,25},{26,2},{2,... | collective-permute-start | bytes 393224 | tf_op jit(solution)/shard_map/while/body/eval_jaxpr/ppermute | solution.py:17
  217.2 4.4 %collective-permute-start.1 = (f32[128,2,128]{2,0,1:T(8,128)S(1)}, f32[128,2,128]{2,0,1:T(8,128)S(1)}, u32[]{:S(2)}, u32[]{:S(2)}) collective-permute-start(f32[128,2,128]{2,0,1:T(8,128)S(1)} %fusion.130), channel_id=1, source_target_pairs={{24,0},{0,8},{8,16},{16,24},{25,1},{1,9},{9,17},{17,25},{26,2},{2,... | collective-permute-start | bytes 393224 | tf_op jit(solution)/shard_map/while/body/eval_jaxpr/ppermute | solution.py:17
  (15 other events, 63.5 us)
where the time goes:
time: 224 us; the launch traced here: 223 us
  waiting for transfers between devices  67.9 us (30%)
  blocking collectives  58.9 us (26%)
  matrix products  40.1 us (18%)
  starting transfers between devices  31 us (14%)
  local copies, waits for them, and re-layouts  19.2 us (9%)
  other arithmetic  4.58 us (2%)
    all_gather x1, blocking collectives, local(): lax.all_gather(grad_state, 'ep', axis=0, tiled=True)  31.4 us
    all_to_all x1, waiting for transfers between devices, local(): lax.all_to_all(send_rows, 'ep', split_axis=0, concat_axis=0, tiled=True)  17.9 us
    all_to_all x1, waiting for transfers between devices, local(): lax.all_to_all(send_grads, 'ep', split_axis=0, concat_axis=0, tiled=True)  17.9 us
    ppermute x12, waiting for transfers between devices, shifted(): return lax.ppermute(block, axis, route)  15.2 us
    all_gather x1, blocking collectives, local(): lax.all_gather(key_rows, 'ctx', axis=0, tiled=True)  13.9 us
    all_gather x1, blocking collectives, local(): lax.all_gather(value_rows, 'ctx', axis=0, tiled=True)  13.6 us
    all_to_all x1, waiting for transfers between devices, local(): lax.all_to_all(partial_value.reshape(ep_count, ctx_count, capacity, model...  11.3 us
    all_to_all x1, starting transfers between devices, local(): lax.all_to_all(send_rows, 'ep', split_axis=0, concat_axis=0, tiled=True)  7.28 us
  transfers between devices with their start and end apart: 18, of which 12 were waited for; matrix products, arithmetic and copies ran while one was open for 13% of the time, Pallas kernels for 0%

commit v1 on v0

--- a/solution.py
+++ b/solution.py
@@ -185,12 +185,20 @@
         up_w,
         down_w,
     )
-    returned = lax.all_to_all(
-        partial_value.reshape(ep_count, ctx_count, capacity, model_width),
-        "ctx",
-        split_axis=1,
-        concat_axis=1,
-        tiled=True,
+    returned = jnp.concatenate(
+        lax.all_to_all(
+            jnp.stack(
+                jnp.split(
+                    partial_value.reshape(ep_count, ctx_count, capacity, model_width),
+                    lax.axis_size("ctx"),
+                    axis=1,
+                )
+            ),
+            "ctx",
+            0,
+            0,
+        ),
+        axis=1,
     )
     returned = lax.all_to_all(returned, "ep", split_axis=0, concat_axis=0, tiled=True)
     summed = jnp.sum(

time: 224 us -> 222 us (level)
    reshape x2 -> x1, local copies, waits for them, and re-layouts: 2.65 us -> 0.26 us  [local(): partial_value.reshape(ep_count, ctx_count, capacity, model_width)]
where the time goes in v1:
time: 222 us
  waiting for transfers between devices  67.9 us (31%)
  blocking collectives  58.9 us (27%)
  matrix products  39.2 us (18%)
  starting transfers between devices  31 us (14%)
  local copies, waits for them, and re-layouts  18.2 us (8%)
  other arithmetic  4.86 us (2%)
    all_gather x1, blocking collectives, local(): lax.all_gather(grad_state, 'ep', axis=0, tiled=True)  31.4 us
    all_to_all x1, waiting for transfers between devices, local(): lax.all_to_all(send_rows, 'ep', split_axis=0, concat_axis=0, tiled=True)  17.9 us
    all_to_all x1, waiting for transfers between devices, local(): lax.all_to_all(send_grads, 'ep', split_axis=0, concat_axis=0, tiled=True)  17.9 us
    ppermute x12, waiting for transfers between devices, shifted(): return lax.ppermute(block, axis, route)  15.2 us
    all_gather x1, blocking collectives, local(): lax.all_gather(key_rows, 'ctx', axis=0, tiled=True)  13.9 us
    all_gather x1, blocking collectives, local(): lax.all_gather(value_rows, 'ctx', axis=0, tiled=True)  13.6 us
    all_to_all x1, waiting for transfers between devices, local(): lax.all_to_all(jnp.stack(jnp.split(partial_value.reshape(ep_count, ctx_co...  11.3 us
    all_to_all x1, starting transfers between devices, local(): lax.all_to_all(send_rows, 'ep', split_axis=0, concat_axis=0, tiled=True)  7.28 us
  transfers between devices with their start and end apart: 18, of which 12 were waited for; matrix products, arithmetic and copies ran while one was open for 13% of the time, Pallas kernels for 0%

profile of v1, /device:TPU:0, one launch (start us, length us, event | category | flops | bytes accessed | tf_op | source)
XLA Modules:
  0.0 221.6 jit_solution(6095270176135750106)
XLA Ops:
  4.6 1.5 copy.122
  6.1 7.3 %all-to-all-start.2 = ((bf16[8,4,6,2048]{3,1,2,0:T(4,128)(2,1)}), bf16[8,4,6,2048]{3,1,2,0:T(4,128)(2,1)}, u32[]{:S(2)}, u32[]{:S(2)}) async-start(bf16[8,4,6,2048]{3,1,2,0:T(4,128)(2,1)} %copy.122), calls=%async_computation.2 | async-start | bytes 1572864 | tf_op jit(solution)/shard_map/all_to_all | solution.py:174
  14.2 1.5 copy.119
  15.7 17.9 %all-to-all-done.2 = bf16[8,4,6,2048]{3,1,2,0:T(4,128)(2,1)} async-done(((bf16[8,4,6,2048]{3,1,2,0:T(4,128)(2,1)}), bf16[8,4,6,2048]{3,1,2,0:T(4,128)(2,1)}, u32[]{:S(2)}, u32[]{:S(2)}) %all-to-all-start.2) | async-done | bytes 786464 | tf_op jit(solution)/shard_map/all_to_all | solution.py:174
  33.6 3.6 %all-to-all-start = ((bf16[8,4,6,2048]{3,1,2,0:T(4,128)(2,1)}), bf16[8,4,6,2048]{3,1,2,0:T(4,128)(2,1)S(1)}, u32[]{:S(2)}, u32[]{:S(2)}) async-start(bf16[8,4,6,2048]{3,1,2,0:T(4,128)(2,1)} %copy.119), calls=%async_computation | async-start | bytes 1572864 | tf_op jit(solution)/shard_map/all_to_all | solution.py:175
  37.2 2.5 %copy.123 = bf16[8,4,6,2048]{3,0,2,1:T(8,128)(2,1)} copy(bf16[8,4,6,2048]{3,1,2,0:T(4,128)(2,1)} %all-to-all-done.2) | data formatting | bytes 1572864 | tf_op jit(solution)/shard_map/all_to_all | solution.py:174
  39.7 17.9 %all-to-all-done = bf16[8,4,6,2048]{3,1,2,0:T(4,128)(2,1)S(1)} async-done(((bf16[8,4,6,2048]{3,1,2,0:T(4,128)(2,1)}), bf16[8,4,6,2048]{3,1,2,0:T(4,128)(2,1)S(1)}, u32[]{:S(2)}, u32[]{:S(2)}) %all-to-all-start) | async-done | bytes 786464 | tf_op jit(solution)/shard_map/all_to_all | solution.py:175
  57.6 3.5 %all-to-all-start.3 = ((bf16[8,4,6,2048]{3,0,2,1:T(8,128)(2,1)}), bf16[8,4,6,2048]{3,0,2,1:T(8,128)(2,1)S(1)}, u32[]{:S(2)}, u32[]{:S(2)}) async-start(bf16[8,4,6,2048]{3,0,2,1:T(8,128)(2,1)} %copy.123), calls=%async_computation.3 | async-start | bytes 1572864 | tf_op jit(solution)/shard_map/all_to_all | solution.py:178
  61.4 13.6 %all_gather.11 = bf16[512,256]{0,1:T(8,128)(2,1)S(1)} all-gather(bf16[128,256]{0,1:T(8,128)(2,1)S(1)} %copy.136), channel_id=1, replica_groups=mesh['ctx'=4,'ep'=8] {'ctx'}, dimensions={0}, use_global_device_ids=true | all-gather | bytes 327680 | tf_op jit(solution)/shard_map/all_gather | solution.py:134
  76.3 4.2 %all-to-all-start.1 = ((bf16[8,4,6,2048]{3,0,2,1:T(8,128)(2,1)}), bf16[8,4,6,2048]{3,0,2,1:T(8,128)(2,1)}, u32[]{:S(2)}, u32[]{:S(2)}) async-start(bf16[8,4,6,2048]{3,0,2,1:T(8,128)(2,1)} %copy.120), calls=%async_computation.1 | async-start | bytes 1572864 | tf_op jit(solution)/shard_map/all_to_all | solution.py:179
  80.5 13.9 %all_gather.10 = bf16[512,256]{0,1:T(8,128)(2,1)S(1)} all-gather(bf16[128,256]{0,1:T(8,128)(2,1)S(1)} %copy.133), channel_id=1, replica_groups=mesh['ctx'=4,'ep'=8] {'ctx'}, dimensions={0}, use_global_device_ids=true | all-gather | bytes 327680 | tf_op jit(solution)/shard_map/all_gather | solution.py:133
  98.0 1.6 copy.121
  100.8 4.7 %fusion.28 = f32[192,1408]{1,0:T(8,128)S(1)} fusion(bf16[192,2048]{1,0:T(8,128)(2,1)S(1)} %copy-done.6, bf16[1,1,1408,2048]{3,2,1,0:T(8,128)(2,1)} %param.19), kind=kOutput, calls=%fused_computation.42 | convolution fusion | flops 1107296256 | bytes 7634944 | tf_op jit(solution)/shard_map/dot_general | solution.py:23
  105.5 5.1 %fusion.32 = f32[192,1408]{1,0:T(8,128)S(1)} fusion(bf16[192,2048]{1,0:T(8,128)(2,1)S(1)} %copy-done.6, bf16[1,1,1408,2048]{3,2,1,0:T(8,128)(2,1)} %param.20), kind=kOutput, calls=%fused_computation.46 | convolution fusion | flops 1107296256 | bytes 7634944 | tf_op jit(solution)/shard_map/dot_general | solution.py:24
  110.7 5.3 %multiply_convert_fusion.1 = (bf16[192,1408]{1,0:T(8,128)(2,1)S(1)}, bf16[192,1408]{1,0:T(8,128)(2,1)S(1)}) fusion(f32[192,1408]{1,0:T(8,128)S(1)} %fusion.28, f32[192,1408]{1,0:T(8,128)S(1)} %fusion.32, bf16[192,2048]{1,0:T(8,128)(2,1)S(1)} %copy-done.8, bf16[1,1,1408,2048]{3,2,1,0:T(8,128)(2,1)} %param.21), kind=kOutput, calls=%fused_computation.62 | convolution fusion | flops 1110810624 | bytes 9797632 | tf_op jit(solution)/shard_map/dot_general | solution.py:27
  117.5 1.4 fusion.39
  120.9 3.5 %all-to-all-start.4 = ((bf16[4,8,1,6,2048]{4,1,3,2,0:T(8,128)(2,1)}), bf16[4,8,1,6,2048]{4,1,3,2,0:T(8,128)(2,1)S(1)}, u32[]{:S(2)}, u32[]{:S(2)}) async-start(bf16[4,8,1,6,2048]{4,1,3,2,0:T(8,128)(2,1)} %copy.128), calls=%async_computation.4 | async-start | bytes 1572864 | tf_op jit(solution)/shard_map/all_to_all | solution.py:189
  124.7 11.3 %all-to-all-done.4 = bf16[4,8,1,6,2048]{4,1,3,2,0:T(8,128)(2,1)S(1)} async-done(((bf16[4,8,1,6,2048]{4,1,3,2,0:T(8,128)(2,1)}), bf16[4,8,1,6,2048]{4,1,3,2,0:T(8,128)(2,1)S(1)}, u32[]{:S(2)}, u32[]{:S(2)}) %all-to-all-start.4) | async-done | bytes 786464 | tf_op jit(solution)/shard_map/all_to_all | solution.py:189
  136.0 1.5 copy.129
  137.5 3.8 %all-to-all-start.5 = ((bf16[8,4,6,2048]{3,1,2,0:T(4,128)(2,1)}), bf16[8,4,6,2048]{3,1,2,0:T(4,128)(2,1)S(1)}, u32[]{:S(2)}, u32[]{:S(2)}) async-start(bf16[8,4,6,2048]{3,1,2,0:T(4,128)(2,1)} %copy.129), calls=%async_computation.5 | async-start | bytes 1572864 | tf_op jit(solution)/shard_map/all_to_all | solution.py:203
  141.4 5.6 %fusion.24 = bf16[1,1,1408,2048]{3,2,1,0:T(8,128)(2,1)} fusion(bf16[192,1408]{1,0:T(8,128)(2,1)} %copy-done.22, bf16[192,2048]{1,0:T(8,128)(2,1)} %reshape.244), kind=kOutput, calls=%fused_computation.38 | convolution fusion | flops 1110179840 | bytes 7094272 | tf_op jit(solution)/shard_map/dot_general | solution.py:39
  147.0 4.2 %fusion.23 = bf16[1,1,1408,2048]{3,2,1,0:T(8,128)(2,1)} fusion(bf16[192,1408]{1,0:T(8,128)(2,1)S(1)} %copy-done.24, bf16[192,2048]{1,0:T(8,128)(2,1)S(1)} %copy-done.7), kind=kOutput, calls=%fused_computation.37 | convolution fusion | flops 1110179840 | bytes 7094272 | tf_op jit(solution)/shard_map/dot_general | solution.py:36
  151.3 4.3 %fusion.25 = bf16[1,1,1408,2048]{3,2,1,0:T(8,128)(2,1)} fusion(bf16[192,2048]{1,0:T(8,128)(2,1)S(1)} %copy-done.9, f32[192,1408]{1,0:T(8,128)S(1)} %copy-done.21, f32[192,1408]{1,0:T(8,128)S(1)} %copy-done.19), kind=kOutput, calls=%fused_computation.39 | convolution fusion | flops 1111801856 | bytes 8716288 | tf_op jit(solution)/shard_map/dot_general | solution.py:40
  155.6 5.5 %all-to-all-done.5 = bf16[8,4,6,2048]{3,1,2,0:T(4,128)(2,1)S(1)} async-done(((bf16[8,4,6,2048]{3,1,2,0:T(4,128)(2,1)}), bf16[8,4,6,2048]{3,1,2,0:T(4,128)(2,1)S(1)}, u32[]{:S(2)}, u32[]{:S(2)}) %all-to-all-start.5) | async-done | bytes 786464 | tf_op jit(solution)/shard_map/all_to_all | solution.py:203
  162.1 31.4 %all_gather.9 = bf16[128,2048]{1,0:T(8,128)(2,1)S(1)} all-gather(bf16[16,2048]{1,0:T(8,128)(2,1)S(1)} %fusion.63), channel_id=1, replica_groups=mesh['ctx'=4,'ep'=8] {'ep'}, dimensions={0}, use_global_device_ids=true | all-gather | bytes 589824 | tf_op jit(solution)/shard_map/all_gather | solution.py:218
  195.0 25.1 %while.22 = (s32[]{:T(128)}, bf16[2,128,2,128]{3,1,2,0:T(8,128)(2,1)S(1)}, f32[128,2,128]{2,0,1:T(8,128)S(1)}, f32[2,2,128]{2,1,0:T(2,128)S(1)}, f32[2,128,2,128...) while((s32[]{:T(128)}, ...), condition=%wide.region_8.9_spmd.clone, body=%wide.region_7.8_spmd.clone.sunk | while | flops 42483984 | bytes 3723668 | solution.py:254
  198.1 2.9 %collective-permute-done.1 = f32[128,2,128]{2,0,1:T(8,128)S(1)} collective-permute-done((f32[128,2,128]{2,0,1:T(8,128)S(1)}, f32[128,2,128]{2,0,1:T(8,128)S(1)}, u32[]{:S(2)}, u32[]{:S(2)}) %collective-permute-start.1) | collective-permute-done | bytes 131104 | tf_op jit(solution)/shard_map/while/body/eval_jaxpr/ppermute | solution.py:17
  201.0 1.5 collective-permute-start
  204.0 3.6 %collective-permute-done.1 = f32[128,2,128]{2,0,1:T(8,128)S(1)} collective-permute-done((f32[128,2,128]{2,0,1:T(8,128)S(1)}, f32[128,2,128]{2,0,1:T(8,128)S(1)}, u32[]{:S(2)}, u32[]{:S(2)}) %collective-permute-start.1) | collective-permute-done | bytes 131104 | tf_op jit(solution)/shard_map/while/body/eval_jaxpr/ppermute | solution.py:17
  210.6 2.9 %collective-permute-done.1 = f32[128,2,128]{2,0,1:T(8,128)S(1)} collective-permute-done((f32[128,2,128]{2,0,1:T(8,128)S(1)}, f32[128,2,128]{2,0,1:T(8,128)S(1)}, u32[]{:S(2)}, u32[]{:S(2)}) %collective-permute-start.1) | collective-permute-done | bytes 131104 | tf_op jit(solution)/shard_map/while/body/eval_jaxpr/ppermute | solution.py:17
  213.5 1.5 collective-permute-start
  216.5 3.6 %collective-permute-done.1 = f32[128,2,128]{2,0,1:T(8,128)S(1)} collective-permute-done((f32[128,2,128]{2,0,1:T(8,128)S(1)}, f32[128,2,128]{2,0,1:T(8,128)S(1)}, u32[]{:S(2)}, u32[]{:S(2)}) %collective-permute-start.1) | collective-permute-done | bytes 131104 | tf_op jit(solution)/shard_map/while/body/eval_jaxpr/ppermute | solution.py:17
  (190 shorter events, 27.5 us)
Async XLA Ops:
  0.6 192.9 %copy-start = (bf16[256,2048]{1,0:T(8,128)(2,1)S(1)}, bf16[256,2048]{1,0:T(8,128)(2,1)}, u32[]{:S(2)}) copy-start(bf16[256,2048]{1,0:T(8,128)(2,1)} %param.22) | copy-start | bytes 3145732
  4.6 8.8 %copy-start.17 = (f32[16,6]{0,1:T(8,128)S(1)}, f32[16,6]{0,1:T(8,128)}, u32[]{:S(2)}) copy-start(f32[16,6]{0,1:T(8,128)} %param.17) | copy-start | bytes 1156
  4.6 9.0 %copy-start.11 = (bf16[16,2048]{1,0:T(8,128)(2,1)S(1)}, bf16[16,2048]{1,0:T(8,128)(2,1)}, u32[]{:S(2)}) copy-start(bf16[16,2048]{1,0:T(8,128)(2,1)} %param.15) | copy-start | bytes 196612
  6.1 27.6 %all-to-all-start.2 = ((bf16[8,4,6,2048]{3,1,2,0:T(4,128)(2,1)}), bf16[8,4,6,2048]{3,1,2,0:T(4,128)(2,1)}, u32[]{:S(2)}, u32[]{:S(2)}) async-start(bf16[8,4,6,2048]{3,1,2,0:T(4,128)(2,1)} %copy.122), calls=%async_computation.2 | async-start | bytes 1572864 | tf_op jit(solution)/shard_map/all_to_all | solution.py:174
  33.6 23.9 %all-to-all-start = ((bf16[8,4,6,2048]{3,1,2,0:T(4,128)(2,1)}), bf16[8,4,6,2048]{3,1,2,0:T(4,128)(2,1)S(1)}, u32[]{:S(2)}, u32[]{:S(2)}) async-start(bf16[8,4,6,2048]{3,1,2,0:T(4,128)(2,1)} %copy.119), calls=%async_computation | async-start | bytes 1572864 | tf_op jit(solution)/shard_map/all_to_all | solution.py:175
  37.2 23.9 %copy-start.2 = (bf16[128,256]{1,0:T(8,128)(2,1)S(1)}, bf16[128,256]{1,0:T(8,128)(2,1)}, u32[]{:S(2)}) copy-start(bf16[128,256]{1,0:T(8,128)(2,1)} %param.24) | copy-start | bytes 196612
  37.2 24.0 %copy-start.1 = (bf16[128,256]{1,0:T(8,128)(2,1)S(1)}, bf16[128,256]{1,0:T(8,128)(2,1)}, u32[]{:S(2)}) copy-start(bf16[128,256]{1,0:T(8,128)(2,1)} %param.25) | copy-start | bytes 196612
  57.6 18.7 %all-to-all-start.3 = ((bf16[8,4,6,2048]{3,0,2,1:T(8,128)(2,1)}), bf16[8,4,6,2048]{3,0,2,1:T(8,128)(2,1)S(1)}, u32[]{:S(2)}, u32[]{:S(2)}) async-start(bf16[8,4,6,2048]{3,0,2,1:T(8,128)(2,1)} %copy.123), calls=%async_computation.3 | async-start | bytes 1572864 | tf_op jit(solution)/shard_map/all_to_all | solution.py:178
  75.0 19.5 %copy-start.10 = (bf16[128,256]{1,0:T(8,128)(2,1)S(1)}, bf16[128,256]{1,0:T(8,128)(2,1)}, u32[]{:S(2)}) copy-start(bf16[128,256]{1,0:T(8,128)(2,1)} %param.23) | copy-start | bytes 196612
  76.3 21.7 %all-to-all-start.1 = ((bf16[8,4,6,2048]{3,0,2,1:T(8,128)(2,1)}), bf16[8,4,6,2048]{3,0,2,1:T(8,128)(2,1)}, u32[]{:S(2)}, u32[]{:S(2)}) async-start(bf16[8,4,6,2048]{3,0,2,1:T(8,128)(2,1)} %copy.120), calls=%async_computation.1 | async-start | bytes 1572864 | tf_op jit(solution)/shard_map/all_to_all | solution.py:179
  105.5 10.5 %slice-start = ((s8[5767168]{0:T(1024)(128)(4,1)}), s8[4194304]{0:T(1024)(128)(4,1)S(1)}, s32[]{:S(2)}) async-start(s8[5767168]{0:T(1024)(128)(4,1)} %bitcast.190), calls=%async_computation.6 | async-start | bytes 8388608
  105.5 12.0 %slice-start.2 = ((s8[5767168]{0:T(1024)(128)(4,1)}), s8[4194304]{0:T(1024)(128)(4,1)S(1)}, s32[]{:S(2)}) async-start(s8[5767168]{0:T(1024)(128)(4,1)} %bitcast.192), calls=%async_computation.8 | async-start | bytes 8388608
  110.7 6.8 %slice-start.3 = ((s8[5767168]{0:T(1024)(128)(4,1)}), s8[1572864]{0:T(1024)(128)(4,1)S(1)}, s32[]{:S(2)}) async-start(s8[5767168]{0:T(1024)(128)(4,1)} %bitcast.192), calls=%async_computation.9 | async-start | bytes 3145728
  120.9 15.1 %all-to-all-start.4 = ((bf16[4,8,1,6,2048]{4,1,3,2,0:T(8,128)(2,1)}), bf16[4,8,1,6,2048]{4,1,3,2,0:T(8,128)(2,1)S(1)}, u32[]{:S(2)}, u32[]{:S(2)}) async-start(bf16[4,8,1,6,2048]{4,1,3,2,0:T(8,128)(2,1)} %copy.128), calls=%async_computation.4 | async-start | bytes 1572864 | tf_op jit(solution)/shard_map/all_to_all | solution.py:189
  137.5 23.6 %all-to-all-start.5 = ((bf16[8,4,6,2048]{3,1,2,0:T(4,128)(2,1)}), bf16[8,4,6,2048]{3,1,2,0:T(4,128)(2,1)S(1)}, u32[]{:S(2)}, u32[]{:S(2)}) async-start(bf16[8,4,6,2048]{3,1,2,0:T(4,128)(2,1)} %copy.129), calls=%async_computation.5 | async-start | bytes 1572864 | tf_op jit(solution)/shard_map/all_to_all | solution.py:203
  151.3 10.5 %copy-start.5 = (bf16[16,2048]{1,0:T(8,128)(2,1)S(1)}, bf16[16,2048]{1,0:T(8,128)(2,1)}, u32[]{:S(2)}) copy-start(bf16[16,2048]{1,0:T(8,128)(2,1)} %param.14) | copy-start | bytes 196612
  151.3 10.5 %copy-start.15 = (f32[2048]{0:T(1024)S(1)}, f32[2048]{0:T(1024)}, u32[]{:S(2)}) copy-start(f32[2048]{0:T(1024)} %param.18) | copy-start | bytes 24580
  151.3 10.6 %copy-start.12 = (bf16[16,2048]{1,0:T(8,128)(2,1)S(1)}, bf16[16,2048]{1,0:T(8,128)(2,1)}, u32[]{:S(2)}) copy-start(bf16[16,2048]{1,0:T(8,128)(2,1)} %param.15) | copy-start | bytes 196612
  161.8 32.4 %copy-start.14 = (bf16[128,256]{0,1:T(8,128)(2,1)S(1)}, bf16[128,256]{0,1:T(8,128)(2,1)}, u32[]{:S(2)}) copy-start(bf16[128,256]{0,1:T(8,128)(2,1)} %copy.131) | copy-start | bytes 196612
  162.1 32.3 %copy-start.13 = (bf16[16,2048]{1,0:T(8,128)(2,1)}, bf16[16,2048]{1,0:T(8,128)(2,1)S(1)}, u32[]{:S(2)}) copy-start(bf16[16,2048]{1,0:T(8,128)(2,1)S(1)} %fusion.63) | copy-start | bytes 196612
  195.0 3.1 %collective-permute-start.2 = (f32[2,2,128]{2,1,0:T(2,128)S(1)}, f32[2,2,128]{2,1,0:T(2,128)S(1)}, u32[]{:S(2)}, u32[]{:S(2)}) collective-permute-start(f32[2,2,128]{2,1,0:T(2,128)S(1)} %copy.205), channel_id=1, source_target_pairs={{24,0},{0,8},{8,16},{16,24},{25,1},{1,9},{9,17},{17,25},{26,2},{2,... | collective-permute-start | bytes 6152 | tf_op jit(solution)/shard_map/while/body/eval_jaxpr/ppermute | solution.py:17
  195.1 5.9 %collective-permute-start = (bf16[2,128,2,128]{3,1,2,0:T(8,128)(2,1)S(1)}, bf16[2,128,2,128]{3,1,2,0:T(8,128)(2,1)S(1)}, u32[]{:S(2)}, u32[]{:S(2)}) collective-permute-start(bf16[2,128,2,128]{3,1,2,0:T(8,128)(2,1)S(1)} %copy.203), channel_id=1, source_target_pairs={{24,0},{0,8},{8,16},{16,24},{25,1},{1,9},{9,17},{17,25},{26,2},{2,... | collective-permute-start | bytes 393224 | tf_op jit(solution)/shard_map/while/body/eval_jaxpr/ppermute | solution.py:17
  196.5 4.5 %collective-permute-start.1 = (f32[128,2,128]{2,0,1:T(8,128)S(1)}, f32[128,2,128]{2,0,1:T(8,128)S(1)}, u32[]{:S(2)}, u32[]{:S(2)}) collective-permute-start(f32[128,2,128]{2,0,1:T(8,128)S(1)} %fusion.130), channel_id=1, source_target_pairs={{24,0},{0,8},{8,16},{16,24},{25,1},{1,9},{9,17},{17,25},{26,2},{2,... | collective-permute-start | bytes 393224 | tf_op jit(solution)/shard_map/while/body/eval_jaxpr/ppermute | solution.py:17
  201.0 3.0 %collective-permute-start.2 = (f32[2,2,128]{2,1,0:T(2,128)S(1)}, f32[2,2,128]{2,1,0:T(2,128)S(1)}, u32[]{:S(2)}, u32[]{:S(2)}) collective-permute-start(f32[2,2,128]{2,1,0:T(2,128)S(1)} %copy.205), channel_id=1, source_target_pairs={{24,0},{0,8},{8,16},{16,24},{25,1},{1,9},{9,17},{17,25},{26,2},{2,... | collective-permute-start | bytes 6152 | tf_op jit(solution)/shard_map/while/body/eval_jaxpr/ppermute | solution.py:17
  201.0 6.6 %collective-permute-start = (bf16[2,128,2,128]{3,1,2,0:T(8,128)(2,1)S(1)}, bf16[2,128,2,128]{3,1,2,0:T(8,128)(2,1)S(1)}, u32[]{:S(2)}, u32[]{:S(2)}) collective-permute-start(bf16[2,128,2,128]{3,1,2,0:T(8,128)(2,1)S(1)} %copy.203), channel_id=1, source_target_pairs={{24,0},{0,8},{8,16},{16,24},{25,1},{1,9},{9,17},{17,25},{26,2},{2,... | collective-permute-start | bytes 393224 | tf_op jit(solution)/shard_map/while/body/eval_jaxpr/ppermute | solution.py:17
  203.1 4.4 %collective-permute-start.1 = (f32[128,2,128]{2,0,1:T(8,128)S(1)}, f32[128,2,128]{2,0,1:T(8,128)S(1)}, u32[]{:S(2)}, u32[]{:S(2)}) collective-permute-start(f32[128,2,128]{2,0,1:T(8,128)S(1)} %fusion.130), channel_id=1, source_target_pairs={{24,0},{0,8},{8,16},{16,24},{25,1},{1,9},{9,17},{17,25},{26,2},{2,... | collective-permute-start | bytes 393224 | tf_op jit(solution)/shard_map/while/body/eval_jaxpr/ppermute | solution.py:17
  207.6 3.0 %collective-permute-start.2 = (f32[2,2,128]{2,1,0:T(2,128)S(1)}, f32[2,2,128]{2,1,0:T(2,128)S(1)}, u32[]{:S(2)}, u32[]{:S(2)}) collective-permute-start(f32[2,2,128]{2,1,0:T(2,128)S(1)} %copy.205), channel_id=1, source_target_pairs={{24,0},{0,8},{8,16},{16,24},{25,1},{1,9},{9,17},{17,25},{26,2},{2,... | collective-permute-start | bytes 6152 | tf_op jit(solution)/shard_map/while/body/eval_jaxpr/ppermute | solution.py:17
  207.6 5.9 %collective-permute-start = (bf16[2,128,2,128]{3,1,2,0:T(8,128)(2,1)S(1)}, bf16[2,128,2,128]{3,1,2,0:T(8,128)(2,1)S(1)}, u32[]{:S(2)}, u32[]{:S(2)}) collective-permute-start(bf16[2,128,2,128]{3,1,2,0:T(8,128)(2,1)S(1)} %copy.203), channel_id=1, source_target_pairs={{24,0},{0,8},{8,16},{16,24},{25,1},{1,9},{9,17},{17,25},{26,2},{2,... | collective-permute-start | bytes 393224 | tf_op jit(solution)/shard_map/while/body/eval_jaxpr/ppermute | solution.py:17
  209.0 4.4 %collective-permute-start.1 = (f32[128,2,128]{2,0,1:T(8,128)S(1)}, f32[128,2,128]{2,0,1:T(8,128)S(1)}, u32[]{:S(2)}, u32[]{:S(2)}) collective-permute-start(f32[128,2,128]{2,0,1:T(8,128)S(1)} %fusion.130), channel_id=1, source_target_pairs={{24,0},{0,8},{8,16},{16,24},{25,1},{1,9},{9,17},{17,25},{26,2},{2,... | collective-permute-start | bytes 393224 | tf_op jit(solution)/shard_map/while/body/eval_jaxpr/ppermute | solution.py:17
  213.5 3.0 %collective-permute-start.2 = (f32[2,2,128]{2,1,0:T(2,128)S(1)}, f32[2,2,128]{2,1,0:T(2,128)S(1)}, u32[]{:S(2)}, u32[]{:S(2)}) collective-permute-start(f32[2,2,128]{2,1,0:T(2,128)S(1)} %copy.205), channel_id=1, source_target_pairs={{24,0},{0,8},{8,16},{16,24},{25,1},{1,9},{9,17},{17,25},{26,2},{2,... | collective-permute-start | bytes 6152 | tf_op jit(solution)/shard_map/while/body/eval_jaxpr/ppermute | solution.py:17
  213.5 6.6 %collective-permute-start = (bf16[2,128,2,128]{3,1,2,0:T(8,128)(2,1)S(1)}, bf16[2,128,2,128]{3,1,2,0:T(8,128)(2,1)S(1)}, u32[]{:S(2)}, u32[]{:S(2)}) collective-permute-start(bf16[2,128,2,128]{3,1,2,0:T(8,128)(2,1)S(1)} %copy.203), channel_id=1, source_target_pairs={{24,0},{0,8},{8,16},{16,24},{25,1},{1,9},{9,17},{17,25},{26,2},{2,... | collective-permute-start | bytes 393224 | tf_op jit(solution)/shard_map/while/body/eval_jaxpr/ppermute | solution.py:17
  215.6 4.4 %collective-permute-start.1 = (f32[128,2,128]{2,0,1:T(8,128)S(1)}, f32[128,2,128]{2,0,1:T(8,128)S(1)}, u32[]{:S(2)}, u32[]{:S(2)}) collective-permute-start(f32[128,2,128]{2,0,1:T(8,128)S(1)} %fusion.130), channel_id=1, source_target_pairs={{24,0},{0,8},{8,16},{16,24},{25,1},{1,9},{9,17},{17,25},{26,2},{2,... | collective-permute-start | bytes 393224 | tf_op jit(solution)/shard_map/while/body/eval_jaxpr/ppermute | solution.py:17
  (15 other events, 61.9 us)
